TPU v7x, 32 devices: a whole 2x2x4 slice. The times are simulated.
32 devices in a mesh: groups: 2 (over y), ctx: 4 (over z), tp: 2 (over x), dp: 2 (over core).
Axes of the slice: x: 2, y: 2, z: 4, core: 2. Of those that a mesh axis runs over, the one named last changes fastest.
Arguments:
- tokens: bfloat16 [1024, 5120], P(('groups', 'ctx'), ('tp', 'dp')), parts along dimension 0, may hold values from -6 to 6
- lengths: int32 [8], P('groups'), parts along dimension 0, may hold values from 1 to 256, 512 in all
- request_adapter_ids: int32 [8], P('groups'), parts along dimension 0, may hold values from 0 to 7
- adapter_store_slot: int32 [8], replicated, may hold values from 0 to 7, each once
- xchan_input_weight: bfloat16 [5120, 4096], P('ctx', ('tp', 'dp')), may hold values from -0.078125 to 0.078125
- bc_input_weight: bfloat16 [5120, 512], P('ctx', ('tp', 'dp')), may hold values from -0.078125 to 0.078125
- step_input_weight: bfloat16 [5120, 64], P('ctx', ('tp', 'dp')), may hold values from -0.078125 to 0.078125
- convolution_x_taps: float32 [4, 4096], P(None, ('tp', 'dp')), may hold values from -3 to 3
- convolution_bc_taps: float32 [4, 512], P(None, ('tp', 'dp')), may hold values from -3 to 3
- step_bias: float32 [64], P(('tp', 'dp')), may hold values from -2 to 1
- decay_log_rate: float32 [64], P(('tp', 'dp')), may hold values from -16 to -2
- head_skip_gain: float32 [64], P(('tp', 'dp')), may hold values from 0.5 to 1.5
- output_norm_gain: float32 [4096], P(('tp', 'dp')), may hold values from 0.1 to 1.9
- output_weight: bfloat16 [4096, 5120], P(('tp', 'dp'), 'ctx'), may hold values from -0.09375 to 0.09375
- adapter_down_input: bfloat16 [8, 5120, 64], P('ctx', ('tp', 'dp')), may hold values from -0.078125 to 0.078125
- adapter_up_xchan: bfloat16 [8, 64, 4096], P('ctx', None, ('tp', 'dp')), may hold values from -0.75 to 0.75
- adapter_up_bc: bfloat16 [8, 64, 512], P('ctx', None, ('tp', 'dp')), may hold values from -0.75 to 0.75
- adapter_down_output: bfloat16 [8, 4096, 64], P('ctx', ('tp', 'dp')), may hold values from -0.09375 to 0.09375
- adapter_up_output: bfloat16 [8, 64, 5120], P('ctx', None, ('tp', 'dp')), may hold values from -0.75 to 0.75
Outputs:
- mixed: bfloat16 [1024, 5120], P(('groups', 'ctx'), ('tp', 'dp')), parts along dimension 0
There are 2 independent parts, one for each index of `groups`. A program takes and returns all parts, laid end to end along the dimension named above; an argument that names none is the same for every part. Nothing has to cross between parts.
Inputs may be any that keep to these rules, and one draw needn't show every extreme that they name: The 4 lengths add up to 512; the longest is exactly 256. `adapter_store_slot`: each slot once; the adapter in slot k is stored on index k // 2 of ctx, at its place k % 2 there.
All inputs are finite; a program needn't handle non-finite values.
Results may differ from a plain program's by a relative error of at most 0.023.
Values may be sent and summed in bfloat16 or wider, within the bound.
No kernel may reach another device: no remote copies, remote signals or barrier semaphores. Data moves between devices by JAX's collectives and lax.ppermute only.
A program may use at most 64 MiB of HBM per device.

v0:
```python
import jax
import jax.numpy as jnp
from jax import lax
from jax.sharding import PartitionSpec as P

FULL_PRECISION = lax.Precision.HIGHEST
NORM_EPSILON = 1e-06


def from_root(block, axis, source):
    block = jnp.where(lax.axis_index(axis) == source, block, jnp.zeros_like(block))
    return lax.psum(block, axis)


def passed_along(shard, axis, by):
    size = lax.axis_size(axis)
    pairs = [(i, i + by) for i in range(size) if 0 <= i + by < size]
    return lax.ppermute(shard, axis, pairs)


def prefix(shard, axis, combine, identity):
    size, place = (lax.axis_size(axis), lax.axis_index(axis))
    everything = jax.tree.map(
        lambda part, kind: lax.all_gather(part.astype(kind), axis),
        shard,
        (jnp.bfloat16, jnp.bfloat16),
    )
    start = jax.tree.map(
        lambda part, zero: jnp.broadcast_to(jnp.asarray(zero, part.dtype), part.shape),
        shard,
        identity,
    )

    def lap(k, before):
        reached = k < place
        new = combine(
            before, jax.tree.map(lambda part, own: part[k].astype(own.dtype), everything, shard)
        )
        return jax.tree.map(lambda a, b: jnp.where(reached, a, b), new, before)

    return lax.fori_loop(0, size, lap, start)


def segment_of(positions, request_ends):
    inside = (positions[:, None] >= request_ends[None, :]).astype(jnp.int32)
    counted = jnp.sum(inside, axis=1, dtype=jnp.int32)
    return jnp.where(positions < 0, jnp.int32(-1), counted)


def span_parts(x_heads, b_proj, c_proj, step_size, log_decay, segment, previous):
    length = x_heads.shape[0]
    cumulative = jnp.cumsum(log_decay, axis=0)
    final_log = cumulative[length - 1]
    places = jnp.arange(length, dtype=jnp.int32)
    same_request = jnp.logical_and(
        segment[:, None] == segment[None, :], places[None, :] <= places[:, None]
    ).astype(jnp.float32)
    log_gap = cumulative.T[:, :, None] - cumulative.T[:, None, :]
    decay_table = jnp.exp(jnp.minimum(log_gap, 0.0)) * same_request[None]
    scores = lax.dot_general(
        c_proj, b_proj, (((1,), (1,)), ((), ())), preferred_element_type=jnp.float32
    )
    weights = scores[None] * decay_table * step_size.T[:, None, :]
    inner_out = jnp.einsum("hts,shd->thd", weights, x_heads, precision=FULL_PRECISION)
    at_end = (segment == segment[length - 1]).astype(jnp.float32)
    state_weight = jnp.exp(final_log[None, :] - cumulative) * at_end[:, None] * step_size
    local_state = jnp.einsum(
        "sh,shd,sn->hdn",
        state_weight,
        x_heads,
        b_proj.astype(jnp.float32),
        precision=FULL_PRECISION,
    )
    enter_weight = jnp.exp(cumulative) * (segment == previous).astype(jnp.float32)[:, None]
    carry_decay = jnp.exp(final_log) * (segment[length - 1] == previous).astype(jnp.float32)
    return (inner_out, local_state, enter_weight, carry_decay)


def select_rows(wide, adapter_picker_matrix):
    shaped = wide.reshape(wide.shape[0], adapter_picker_matrix.shape[1], -1)
    return jnp.sum(shaped * adapter_picker_matrix[:, :, None], axis=1)


def masked_wide(values, onehot_b):
    return (values[:, None, :] * onehot_b[:, :, None]).reshape(values.shape[0], -1)


def body(
    tokens,
    lengths,
    request_adapter_ids,
    adapter_store_slot,
    xchan_input_weight,
    bc_input_weight,
    step_input_weight,
    convolution_x_taps,
    convolution_bc_taps,
    step_bias,
    decay_log_rate,
    head_skip_gain,
    output_norm_gain,
    output_weight,
    adapter_down_input,
    adapter_up_xchan,
    adapter_up_bc,
    adapter_down_output,
    adapter_up_output,
):
    length = tokens.shape[0]
    request_list = lengths.shape[0]
    taps = convolution_x_taps.shape[0]
    bank_entries = adapter_down_input.shape[0]
    head_count = step_bias.shape[0]
    channels = xchan_input_weight.shape[1]
    start_pos = lax.axis_index("ctx") * length
    request_ends = jnp.cumsum(lengths, dtype=jnp.int32)
    positions = start_pos + jnp.arange(length, dtype=jnp.int32)
    segment = segment_of(positions, request_ends)
    previous = segment_of(jnp.reshape(start_pos - 1, (1,)), request_ends)[0]
    adapter_picker_matrix = (
        segment[:, None] == jnp.arange(request_list, dtype=jnp.int32)[None, :]
    ).astype(jnp.float32)
    onehot_b = adapter_picker_matrix.astype(jnp.bfloat16)
    slot_indices = adapter_store_slot[request_adapter_ids]
    initial_stacks = (
        jnp.zeros(
            (adapter_down_input.shape[1], request_list, adapter_down_input.shape[2]), jnp.bfloat16
        ),
        jnp.zeros((request_list,) + adapter_up_xchan.shape[1:], jnp.bfloat16),
        jnp.zeros((request_list,) + adapter_up_bc.shape[1:], jnp.bfloat16),
        jnp.zeros(
            (adapter_down_output.shape[1], request_list, adapter_down_output.shape[2]), jnp.bfloat16
        ),
        jnp.zeros((request_list,) + adapter_up_output.shape[1:], jnp.bfloat16),
    )
    stack_dims = (1, 0, 0, 1, 0)

    def fetch(request_item, current):
        slot = slot_indices[request_item]
        owner = slot // bank_entries
        within = slot % bank_entries
        a_in, b_x, b_bc, a_out, b_out = [
            lax.dynamic_index_in_dim(adapter_bank, within, 0, keepdims=False)
            for adapter_bank in (
                adapter_down_input,
                adapter_up_xchan,
                adapter_up_bc,
                adapter_down_output,
                adapter_up_output,
            )
        ]
        received = (
            from_root(a_in, "ctx", owner),
            from_root(b_x, "ctx", owner),
            from_root(b_bc, "ctx", owner),
            from_root(a_out, "ctx", owner),
            from_root(b_out, "ctx", owner),
        )
        return tuple(
            (
                lax.dynamic_update_index_in_dim(stack, panel, request_item, along)
                for stack, panel, along in zip(current, received, stack_dims)
            )
        )

    stacks = lax.fori_loop(0, request_list, fetch, initial_stacks)
    rank_value = adapter_down_input.shape[2]
    down_in = stacks[0].reshape(stacks[0].shape[0], request_list * rank_value)
    up_x = stacks[1].reshape(request_list * rank_value, -1)
    up_bc = stacks[2].reshape(request_list * rank_value, -1)
    down_out = stacks[3].reshape(stacks[3].shape[0], request_list * rank_value)
    up_out = stacks[4].reshape(request_list * rank_value, -1)
    lowrank_part = select_rows(
        jnp.dot(tokens, down_in, preferred_element_type=jnp.float32), adapter_picker_matrix
    )
    rank_hidden = lax.psum(lowrank_part.astype(jnp.bfloat16), ("tp", "dp"))
    lowrank_wide = masked_wide(rank_hidden, onehot_b)
    full_tokens = lax.all_gather(tokens, ("tp", "dp"), axis=1, tiled=True)
    pieces = (
        lax.all_gather(xchan_input_weight, "ctx", axis=0, tiled=True),
        lax.all_gather(bc_input_weight, "ctx", axis=0, tiled=True),
        lax.all_gather(step_input_weight, "ctx", axis=0, tiled=True),
    )
    xchan_values, bc_channel_values, step_raw = tuple(
        (jnp.dot(full_tokens, piece, preferred_element_type=jnp.float32) for piece in pieces)
    )
    xchan_values = xchan_values + jnp.dot(lowrank_wide, up_x, preferred_element_type=jnp.float32)
    bc_channel_values = bc_channel_values + jnp.dot(
        lowrank_wide, up_bc, preferred_element_type=jnp.float32
    )
    values = jnp.concatenate([xchan_values, bc_channel_values], axis=1)
    kernel = jnp.concatenate([convolution_x_taps, convolution_bc_taps], axis=1)
    tail_rows = passed_along(values[length - (taps - 1) :], "ctx", 1)
    extended = jnp.concatenate([tail_rows, values], axis=0)
    extended_segment = segment_of(
        start_pos - (taps - 1) + jnp.arange(length + taps - 1, dtype=jnp.int32), request_ends
    )
    convolved = jnp.zeros_like(values)
    for tap in range(taps):
        keep = (extended_segment[tap : tap + length] == segment).astype(jnp.float32)
        convolved = convolved + kernel[tap][None, :] * extended[tap : tap + length] * keep[:, None]
    act = jax.nn.silu(convolved)
    x_heads = act[:, :channels].reshape(length, head_count, -1)
    bc_local = act[:, channels:].astype(jnp.bfloat16)
    bc_all = lax.all_gather(bc_local, ("tp", "dp"), axis=1, tiled=True)
    state_width = bc_all.shape[1] // 2
    b_proj = bc_all[:, :state_width]
    c_proj = bc_all[:, state_width:]
    step_size = jax.nn.softplus(step_raw + step_bias[None, :])
    log_decay = -step_size * jnp.exp(decay_log_rate)[None, :]
    inner_out, local_state, enter_weight, carry_decay = span_parts(
        x_heads, b_proj, c_proj, step_size, log_decay, segment, previous
    )

    def compose(earlier, later):
        return (earlier[0] * later[0], later[0][:, None, None] * earlier[1] + later[1])

    carried = prefix(
        (carry_decay, local_state),
        "ctx",
        compose,
        (jnp.ones_like(carry_decay), jnp.zeros_like(local_state)),
    )
    entering = carried[1]
    entered = (
        jnp.einsum("tn,hdn->thd", c_proj.astype(jnp.float32), entering, precision=FULL_PRECISION)
        * enter_weight[:, :, None]
    )
    mixer_out = (inner_out + entered + head_skip_gain[None, :, None] * x_heads).reshape(
        length, channels
    )
    scale = lax.rsqrt(jnp.mean(mixer_out * mixer_out, axis=1, keepdims=True) + NORM_EPSILON)
    normalized_rows = (mixer_out * scale * output_norm_gain[None, :]).astype(jnp.bfloat16)
    term = jnp.dot(
        normalized_rows,
        lax.all_gather(output_weight, "ctx", axis=1, tiled=True),
        preferred_element_type=jnp.float32,
    )
    base = lax.psum_scatter(
        term.astype(jnp.bfloat16), ("tp", "dp"), scatter_dimension=1, tiled=True
    ).astype(jnp.float32)
    lowrank_out_part = select_rows(
        jnp.dot(normalized_rows, down_out, preferred_element_type=jnp.float32),
        adapter_picker_matrix,
    )
    rank_hidden_output = lax.psum(lowrank_out_part.astype(jnp.bfloat16), ("tp", "dp"))
    adapter_term = jnp.dot(
        masked_wide(rank_hidden_output, onehot_b), up_out, preferred_element_type=jnp.float32
    )
    return (base + adapter_term).astype(jnp.bfloat16)


def solution(mesh):
    placed = (
        P(("groups", "ctx"), ("tp", "dp")),
        P("groups"),
        P("groups"),
        P(),
        P("ctx", ("tp", "dp")),
        P("ctx", ("tp", "dp")),
        P("ctx", ("tp", "dp")),
        P(None, ("tp", "dp")),
        P(None, ("tp", "dp")),
        P(("tp", "dp")),
        P(("tp", "dp")),
        P(("tp", "dp")),
        P(("tp", "dp")),
        P(("tp", "dp"), "ctx"),
        P("ctx", ("tp", "dp"), None),
        P("ctx", None, ("tp", "dp")),
        P("ctx", None, ("tp", "dp")),
        P("ctx", ("tp", "dp"), None),
        P("ctx", None, ("tp", "dp")),
    )
    return jax.shard_map(
        body,
        mesh=mesh,
        in_specs=placed,
        out_specs=P(("groups", "ctx"), ("tp", "dp")),
        check_vma=False,
    )
```

profile of v0, /device:TPU:0, one launch (start us, length us, event | category | flops | bytes accessed | tf_op | source)
XLA Modules:
  0.0 752.0 jit_solution(9867855290832250756)
XLA Ops:
  8.7 217.9 %while.37 = (s32[]{:T(128)}, bf16[1280,4,64]{0,2,1:T(8,128)(2,1)S(1)}, bf16[4,64,1024]{2,1,0:T(8,128)(2,1)S(1)}, bf16[4,64,128]{2,1,0:T(8,128)(2,1)S(1)}, bf16[1...) while((s32[]{:T(128)}, ...), condition=%wide.region_6.7_spmd, body=%wide.region_0.6_spmd.sunk | while | flops 606236 | bytes 6128176 | solution.py:166
  11.9 1.6 dynamic-slice_select_fusion.7
  13.5 1.6 select_bitcast_fusion.4
  15.1 1.6 dynamic-slice_select_fusion.6
  16.7 1.6 select_bitcast_fusion.5
  18.3 20.5 %psum.87 = bf16[1,64,128]{2,1,0:T(8,128)(2,1)S(1)} all-reduce(bf16[1,64,128]{2,1,0:T(8,128)(2,1)S(1)} %dynamic-slice_select_fusion.8), channel_id=1, replica_groups=mesh['groups'=2,'ctx'=4,'tp'=2,'dp'=2] {'ctx'}, use_global_device_ids=true, to_apply=%region_3.3 | all-reduce | flops 8192 | bytes 32768 | tf_op jit(solution)/shard_map/while/body/eval_jaxpr/psum | solution.py:12
  38.8 22.3 %all-reduce.5.cloned.1.call-done = (bf16[1280,1,64]{0,2,1:T(8,128)(2,1)}, bf16[1,64,1024]{2,1,0:T(8,128)(2,1)}, bf16[1024,1,64]{0,2,1:T(8,128)(2,1)}, bf16[1,64,1280]{2,1,0:T(8,128)(2,1)}) async-done(((bf16[1280,1,64]{0,2,1:T(8,128)(2,1)}, bf16[1,64,1024]{2,1,0:T(8,128)(2,1)}, bf16[1024,1,64]{0,2,1:T(8,128)(2,1)}, bf16[1,64,1280]{2,1,0:T(8,128)(2,1)}), (bf16[1280,1,64]{0,2,1:T(8,128)(2,1)}, ...) | async-done | bytes 589840 | tf_op jit(solution)/shard_map/while/body/eval_jaxpr/psum | solution.py:12
  63.9 1.6 constant_dynamic-update-slice_fusion.15
  68.7 1.6 dynamic-slice_select_fusion.7
  70.3 1.6 select_bitcast_fusion.4
  71.9 1.6 dynamic-slice_select_fusion.6
  73.5 1.6 select_bitcast_fusion.5
  75.1 17.3 %psum.87 = bf16[1,64,128]{2,1,0:T(8,128)(2,1)S(1)} all-reduce(bf16[1,64,128]{2,1,0:T(8,128)(2,1)S(1)} %dynamic-slice_select_fusion.8), channel_id=1, replica_groups=mesh['groups'=2,'ctx'=4,'tp'=2,'dp'=2] {'ctx'}, use_global_device_ids=true, to_apply=%region_3.3 | all-reduce | flops 8192 | bytes 32768 | tf_op jit(solution)/shard_map/while/body/eval_jaxpr/psum | solution.py:12
  92.4 22.4 %all-reduce.5.cloned.1.call-done = (bf16[1280,1,64]{0,2,1:T(8,128)(2,1)}, bf16[1,64,1024]{2,1,0:T(8,128)(2,1)}, bf16[1024,1,64]{0,2,1:T(8,128)(2,1)}, bf16[1,64,1280]{2,1,0:T(8,128)(2,1)}) async-done(((bf16[1280,1,64]{0,2,1:T(8,128)(2,1)}, bf16[1,64,1024]{2,1,0:T(8,128)(2,1)}, bf16[1024,1,64]{0,2,1:T(8,128)(2,1)}, bf16[1,64,1280]{2,1,0:T(8,128)(2,1)}), (bf16[1280,1,64]{0,2,1:T(8,128)(2,1)}, ...) | async-done | bytes 589840 | tf_op jit(solution)/shard_map/while/body/eval_jaxpr/psum | solution.py:12
  117.6 1.6 constant_dynamic-update-slice_fusion.15
  122.4 1.6 dynamic-slice_select_fusion.7
  124.0 1.6 select_bitcast_fusion.4
  125.6 1.6 dynamic-slice_select_fusion.6
  127.2 1.6 select_bitcast_fusion.5
  128.8 17.3 %psum.87 = bf16[1,64,128]{2,1,0:T(8,128)(2,1)S(1)} all-reduce(bf16[1,64,128]{2,1,0:T(8,128)(2,1)S(1)} %dynamic-slice_select_fusion.8), channel_id=1, replica_groups=mesh['groups'=2,'ctx'=4,'tp'=2,'dp'=2] {'ctx'}, use_global_device_ids=true, to_apply=%region_3.3 | all-reduce | flops 8192 | bytes 32768 | tf_op jit(solution)/shard_map/while/body/eval_jaxpr/psum | solution.py:12
  146.1 22.4 %all-reduce.5.cloned.1.call-done = (bf16[1280,1,64]{0,2,1:T(8,128)(2,1)}, bf16[1,64,1024]{2,1,0:T(8,128)(2,1)}, bf16[1024,1,64]{0,2,1:T(8,128)(2,1)}, bf16[1,64,1280]{2,1,0:T(8,128)(2,1)}) async-done(((bf16[1280,1,64]{0,2,1:T(8,128)(2,1)}, bf16[1,64,1024]{2,1,0:T(8,128)(2,1)}, bf16[1024,1,64]{0,2,1:T(8,128)(2,1)}, bf16[1,64,1280]{2,1,0:T(8,128)(2,1)}), (bf16[1280,1,64]{0,2,1:T(8,128)(2,1)}, ...) | async-done | bytes 589840 | tf_op jit(solution)/shard_map/while/body/eval_jaxpr/psum | solution.py:12
  171.3 1.6 constant_dynamic-update-slice_fusion.15
  176.1 1.6 dynamic-slice_select_fusion.7
  177.7 1.6 select_bitcast_fusion.4
  179.3 1.6 dynamic-slice_select_fusion.6
  180.8 1.6 select_bitcast_fusion.5
  182.5 17.3 %psum.87 = bf16[1,64,128]{2,1,0:T(8,128)(2,1)S(1)} all-reduce(bf16[1,64,128]{2,1,0:T(8,128)(2,1)S(1)} %dynamic-slice_select_fusion.8), channel_id=1, replica_groups=mesh['groups'=2,'ctx'=4,'tp'=2,'dp'=2] {'ctx'}, use_global_device_ids=true, to_apply=%region_3.3 | all-reduce | flops 8192 | bytes 32768 | tf_op jit(solution)/shard_map/while/body/eval_jaxpr/psum | solution.py:12
  199.8 22.4 %all-reduce.5.cloned.1.call-done = (bf16[1280,1,64]{0,2,1:T(8,128)(2,1)}, bf16[1,64,1024]{2,1,0:T(8,128)(2,1)}, bf16[1024,1,64]{0,2,1:T(8,128)(2,1)}, bf16[1,64,1280]{2,1,0:T(8,128)(2,1)}) async-done(((bf16[1280,1,64]{0,2,1:T(8,128)(2,1)}, bf16[1,64,1024]{2,1,0:T(8,128)(2,1)}, bf16[1024,1,64]{0,2,1:T(8,128)(2,1)}, bf16[1,64,1280]{2,1,0:T(8,128)(2,1)}), (bf16[1280,1,64]{0,2,1:T(8,128)(2,1)}, ...) | async-done | bytes 589840 | tf_op jit(solution)/shard_map/while/body/eval_jaxpr/psum | solution.py:12
  225.0 1.6 constant_dynamic-update-slice_fusion.15
  231.5 11.7 %psum.84 = bf16[128,64]{0,1:T(8,128)(2,1)S(1)} all-reduce(bf16[128,64]{0,1:T(8,128)(2,1)S(1)} %multiply_reduce_fusion.1), channel_id=1, replica_groups=mesh['groups'=2,'ctx'=4,'tp'=2,'dp'=2] {'tp','dp'}, use_global_device_ids=true, to_apply=%region_10.11 | all-reduce | flops 8192 | bytes 32768 | tf_op jit(solution)/shard_map/psum | solution.py:176
  243.2 13.8 %all_gather.32 = bf16[5120,16]{0,1:T(8,128)(2,1)S(1)} all-gather(bf16[1280,16]{0,1:T(8,128)(2,1)S(1)} %copy-done.5), channel_id=1, replica_groups=mesh['groups'=2,'ctx'=4,'tp'=2,'dp'=2] {'ctx'}, dimensions={0}, use_global_device_ids=true | all-gather | bytes 204800 | tf_op jit(solution)/shard_map/all_gather | solution.py:182
  258.3 1.9 compare_select_fusion
  260.6 19.5 %all-gather.12.cloned.1.call-done = bf16[5120,128]{1,0:T(8,128)(2,1)} async-done(((bf16[1280,128]{1,0:T(8,128)(2,1)}), bf16[5120,128]{1,0:T(8,128)(2,1)}) %all-gather.12.cloned.1.call-update) | async-done | bytes 1310736 | tf_op jit(solution)/shard_map/all_gather | solution.py:181
  280.1 1.8 convolution_add_fusion.1
  282.0 182.5 %all-gather.10.cloned.1.call-done = bf16[5120,1024]{1,0:T(8,128)(2,1)} async-done(((bf16[1280,1024]{1,0:T(8,128)(2,1)}), bf16[5120,1024]{1,0:T(8,128)(2,1)}) %all-gather.10.cloned.1.call-update) | async-done | bytes 10485776 | tf_op jit(solution)/shard_map/all_gather | solution.py:180
  464.5 5.6 convolution_add_fusion
  471.5 1.4 collective-permute-done
  473.6 5.4 all_gather.31
  479.1 1.4 convolution_convert_fusion.1
  481.4 10.7 %all-gather.1 = bf16[4,1,16]{2,1,0:T(2,128)(2,1)S(1)} all-gather(bf16[1,1,16]{2,1,0:T(2,128)(2,1)S(1)} %get-tuple-element.473), channel_id=1, replica_groups=mesh['groups'=2,'ctx'=4,'tp'=2,'dp'=2] {'ctx'}, dimensions={0}, use_global_device_ids=true | all-gather | bytes 160 | tf_op jit(solution)/shard_map/all_gather | solution.py:24
  492.5 2.3 convolution_bitcast_fusion.1
  494.8 32.5 %all-gather.16.cloned.1.call-done = bf16[64,64,256]{2,1,0:T(8,128)(2,1)} async-done(((bf16[16,64,256]{2,1,0:T(8,128)(2,1)}), bf16[64,64,256]{2,1,0:T(8,128)(2,1)}) %all-gather.16.cloned.1.call-update) | async-done | bytes 2097168 | tf_op jit(solution)/shard_map/all_gather | solution.py:24
  527.3 5.4 while.38
  533.5 177.9 %all-gather.14.cloned.1.call-done = bf16[1024,5120]{1,0:T(8,128)(2,1)} async-done(((bf16[1024,1280]{1,0:T(8,128)(2,1)}), bf16[1024,5120]{1,0:T(8,128)(2,1)}) %all-gather.14.cloned.1.call-update) | async-done | bytes 10485776 | tf_op jit(solution)/shard_map/all_gather | solution.py:236
  711.5 6.6 convolution_convert_fusion
  719.4 11.2 %psum.85 = bf16[128,64]{0,1:T(8,128)(2,1)S(1)} all-reduce(bf16[128,64]{0,1:T(8,128)(2,1)S(1)} %fusion.5), channel_id=1, replica_groups=mesh['groups'=2,'ctx'=4,'tp'=2,'dp'=2] {'tp','dp'}, use_global_device_ids=true, to_apply=%region_19.20 | all-reduce | flops 8192 | bytes 32768 | tf_op jit(solution)/shard_map/psum | solution.py:246
  730.6 12.3 %reduce-scatter.2.cloned.1.call-done = bf16[128,1280]{1,0:T(8,128)(2,1)} async-done(((bf16[128,5120]{1,0:T(8,128)(2,1)}), bf16[128,1280]{1,0:T(8,128)(2,1)}) %reduce-scatter.2.cloned.1.call-update) | async-done | bytes 327696 | tf_op jit(solution)/shard_map/reduce_scatter | solution.py:239
  742.9 2.0 fusion.2
  (138 shorter events, 31.1 us)
Async XLA Ops:
  7.4 0.7 copy-start
  8.7 9.6 %copy-start.4 = (bf16[2,64,128]{2,1,0:T(8,128)(2,1)S(1)}, bf16[2,64,128]{2,1,0:T(8,128)(2,1)}, u32[]{:S(2)}) copy-start(bf16[2,64,128]{2,1,0:T(8,128)(2,1)} %get-tuple-element.642) | copy-start | bytes 98308 | tf_op jit(solution)/shard_map/while
  8.7 52.5 %all-reduce.5.cloned.1.call-start = ((), (), s32[]{:S(2)}) async-start(), calls=%async_computation.7 | async-start | bytes 1179648 | tf_op jit(solution)/shard_map/while/body/eval_jaxpr/psum | solution.py:12
  65.5 9.5 %copy-start.4 = (bf16[2,64,128]{2,1,0:T(8,128)(2,1)S(1)}, bf16[2,64,128]{2,1,0:T(8,128)(2,1)}, u32[]{:S(2)}) copy-start(bf16[2,64,128]{2,1,0:T(8,128)(2,1)} %get-tuple-element.642) | copy-start | bytes 98308 | tf_op jit(solution)/shard_map/while
  65.5 49.3 %all-reduce.5.cloned.1.call-start = ((), (), s32[]{:S(2)}) async-start(), calls=%async_computation.7 | async-start | bytes 1179648 | tf_op jit(solution)/shard_map/while/body/eval_jaxpr/psum | solution.py:12
  119.2 9.5 %copy-start.4 = (bf16[2,64,128]{2,1,0:T(8,128)(2,1)S(1)}, bf16[2,64,128]{2,1,0:T(8,128)(2,1)}, u32[]{:S(2)}) copy-start(bf16[2,64,128]{2,1,0:T(8,128)(2,1)} %get-tuple-element.642) | copy-start | bytes 98308 | tf_op jit(solution)/shard_map/while
  119.2 49.3 %all-reduce.5.cloned.1.call-start = ((), (), s32[]{:S(2)}) async-start(), calls=%async_computation.7 | async-start | bytes 1179648 | tf_op jit(solution)/shard_map/while/body/eval_jaxpr/psum | solution.py:12
  172.9 9.5 %copy-start.4 = (bf16[2,64,128]{2,1,0:T(8,128)(2,1)S(1)}, bf16[2,64,128]{2,1,0:T(8,128)(2,1)}, u32[]{:S(2)}) copy-start(bf16[2,64,128]{2,1,0:T(8,128)(2,1)} %get-tuple-element.642) | copy-start | bytes 98308 | tf_op jit(solution)/shard_map/while
  172.9 49.3 %all-reduce.5.cloned.1.call-start = ((), (), s32[]{:S(2)}) async-start(), calls=%async_computation.7 | async-start | bytes 1179648 | tf_op jit(solution)/shard_map/while/body/eval_jaxpr/psum | solution.py:12
  226.6 31.7 %all-gather.8.cloned.1.call-start = ((), (), s32[]{:S(2)}) async-start(), calls=%async_computation.1 | async-start | bytes 1638400 | tf_op jit(solution)/shard_map/all_gather | solution.py:178
  227.1 53.0 %all-gather.12.cloned.1.call-start = ((), (), s32[]{:S(2)}) async-start(), calls=%async_computation.3 | async-start | bytes 1638400 | tf_op jit(solution)/shard_map/all_gather | solution.py:181
  227.7 0.7 copy-start.11
  227.7 3.4 copy-start.12
  227.7 3.4 copy-start.2
  227.8 236.7 %all-gather.10.cloned.1.call-start = ((), (), s32[]{:S(2)}) async-start(), calls=%async_computation.2 | async-start | bytes 13107200 | tf_op jit(solution)/shard_map/all_gather | solution.py:180
  228.3 14.9 %copy-start.5 = (bf16[1280,16]{0,1:T(8,128)(2,1)S(1)}, bf16[1280,16]{0,1:T(8,128)(2,1)}, u32[]{:S(2)}) copy-start(bf16[1280,16]{0,1:T(8,128)(2,1)} %param.29) | copy-start | bytes 122884
  228.3 28.7 %copy-start.7 = (f32[4,1024]{1,0:T(4,128)S(1)}, f32[4,1024]{1,0:T(4,128)}, u32[]{:S(2)}) copy-start(f32[4,1024]{1,0:T(4,128)} %param.30) | copy-start | bytes 49156
  228.4 28.7 %copy-start.8 = (f32[4,128]{1,0:T(4,128)S(1)}, f32[4,128]{1,0:T(4,128)}, u32[]{:S(2)}) copy-start(f32[4,128]{1,0:T(4,128)} %param.31) | copy-start | bytes 6148
  228.4 298.9 %all-gather.16.cloned.1.call-start = ((), (), s32[]{:S(2)}) async-start(), calls=%async_computation.6 | async-start | bytes 2621440 | tf_op jit(solution)/shard_map/all_gather | solution.py:24
  231.1 27.2 %copy-start.9 = (f32[16]{0:T(128)S(1)}, f32[16]{0:T(128)}, u32[]{:S(2)}) copy-start(f32[16]{0:T(128)} %param.32) | copy-start | bytes 196
  258.3 21.8 %copy-start.1 = (bf16[128,5120]{1,0:T(8,128)(2,1)S(1)}, bf16[128,5120]{1,0:T(8,128)(2,1)}, u32[]{:S(2)}) copy-start(bf16[128,5120]{1,0:T(8,128)(2,1)} %all-gather.8.cloned.1.call-done) | copy-start | bytes 3932164
  470.1 2.7 collective-permute-start
  480.5 231.0 %all-gather.14.cloned.1.call-start = ((), (), s32[]{:S(2)}) async-start(), calls=%async_computation.4 | async-start | bytes 13107200 | tf_op jit(solution)/shard_map/all_gather | solution.py:236
  481.3 261.6 %reduce-scatter.2.cloned.1.call-start = ((), (), s32[]{:S(2)}) async-start(), calls=%async_computation.5 | async-start | bytes 1638400 | tf_op jit(solution)/shard_map/reduce_scatter | solution.py:239
  527.3 5.4 copy-start.10
  532.6 0.7 copy-start.6
  718.1 1.0 copy-start.3
Sparse Core Ops, SparseCore 0:
  18.4 42.7 all-reduce.4
  75.2 39.6 all-reduce.4
  128.9 39.6 all-reduce.4
  182.5 39.6 all-reduce.4
Sparse Core Ops, SparseCore 1:
  228.6 17.6 all-gather.7
  247.7 32.4 all-gather.11
  281.6 182.8 all-gather.9
  480.6 46.6 all-gather.15
  528.9 182.5 all-gather.13
  718.2 24.6 reduce-scatter.1
where the time goes:
time: 754 us; the launch traced here: 752 us
  waiting for transfers between devices  518 us (69%)
  blocking collectives  125 us (17%)
  other arithmetic  34.3 us (5%)
  matrix products  23.5 us (3%)
  local copies, waits for them, and re-layouts  22.5 us (3%)
  between operations  16.1 us (2%)
  loops' own time  10.7 us (1%)
    all_gather x1, waiting for transfers between devices, body(): lax.all_gather(xchan_input_weight, 'ctx', axis=0, tiled=True)  182 us
    all_gather x1, waiting for transfers between devices, body(): lax.all_gather(output_weight, 'ctx', axis=1, tiled=True)  178 us
    psum x4, waiting for transfers between devices, from_root(): return lax.psum(block, axis)  89.6 us
    psum x4, blocking collectives, from_root(): return lax.psum(block, axis)  72.5 us
    all_gather x1, waiting for transfers between devices, prefix(): lax.all_gather(part.astype(kind), axis)  32.5 us
    all_gather x1, waiting for transfers between devices, body(): lax.all_gather(bc_input_weight, 'ctx', axis=0, tiled=True)  19.5 us
    dynamic_update_slice x20, local copies, waits for them, and re-layouts, fetch(): lax.dynamic_update_index_in_dim(stack, panel, request_item, along)  17.5 us
  transfers between devices with their start and end apart: 11, of which 10 were waited for; matrix products, arithmetic and copies ran while one was open for 2% of the time, Pallas kernels for 0%

commit v1 on v0

--- a/solution.py
+++ b/solution.py
@@ -5,6 +5,18 @@
 
 FULL_PRECISION = lax.Precision.HIGHEST
 NORM_EPSILON = 1e-06
+
+
+def doubled_up(x, axis, dim):
+    ways, here = (lax.axis_size(axis), lax.axis_index(axis))
+    grown, reach = (x, 1)
+    while reach < ways:
+        theirs = lax.ppermute(grown, axis, [(d, d ^ reach) for d in range(ways)])
+        mine_first = jnp.concatenate([grown, theirs], axis=dim)
+        theirs_first = jnp.concatenate([theirs, grown], axis=dim)
+        grown = jnp.where(here & reach == 0, mine_first, theirs_first)
+        reach = 2 * reach
+    return grown
 
 
 def from_root(block, axis, source):
@@ -232,9 +244,7 @@
     scale = lax.rsqrt(jnp.mean(mixer_out * mixer_out, axis=1, keepdims=True) + NORM_EPSILON)
     normalized_rows = (mixer_out * scale * output_norm_gain[None, :]).astype(jnp.bfloat16)
     term = jnp.dot(
-        normalized_rows,
-        lax.all_gather(output_weight, "ctx", axis=1, tiled=True),
-        preferred_element_type=jnp.float32,
+        normalized_rows, doubled_up(output_weight, "ctx", 1), preferred_element_type=jnp.float32
     )
     base = lax.psum_scatter(
         term.astype(jnp.bfloat16), ("tp", "dp"), scatter_dimension=1, tiled=True

time: 754 us -> 833 us (1.10)
  blocking collectives: 125 us -> 313 us
  waiting for transfers between devices: 518 us -> 387 us
  other arithmetic: 34.3 us -> 47.4 us
    all_gather x1 -> x0, waiting for transfers between devices: 178 us -> none  [body(): lax.all_gather(output_weight, 'ctx', axis=1, tiled=True)]
    all_gather x1, blocking collectives: 10.7 us -> 139 us  [prefix(): lax.all_gather(part.astype(kind), axis)]
    ppermute x0 -> x2, waiting for transfers between devices: none -> 89 us  [doubled_up(): theirs = lax.ppermute(grown, axis, [(d, d ^ reach) for d in range(ways)])]
    all_gather x1, blocking collectives: 13.8 us -> 73.3 us  [body(): lax.all_gather(step_input_weight, 'ctx', axis=0, tiled=True)]
    all_gather x1, waiting for transfers between devices: 182 us -> 163 us  [body(): lax.all_gather(xchan_input_weight, 'ctx', axis=0, tiled=True)]
    all_gather x1, waiting for transfers between devices: 19.5 us -> 0.01 us  [body(): lax.all_gather(bc_input_weight, 'ctx', axis=0, tiled=True)]
    reduce_scatter x1, waiting for transfers between devices: 12.3 us -> 24.5 us  [body(): lax.psum_scatter(term.astype(jnp.bfloat16), ('tp', 'dp'), scatter_dimensi...]
    all_gather x1, waiting for transfers between devices: 32.5 us -> 21.9 us  [prefix(): lax.all_gather(part.astype(kind), axis)]
  transfers between devices with their start and end apart: 11 -> 12, of which waited for: 10 -> 9; matrix products, arithmetic and copies ran while one was open for 2% -> 4% of each run, Pallas kernels for 0% -> 0%
where the time goes in v1:
time: 833 us; the launch traced here: 831 us
  waiting for transfers between devices  387 us (46%)
  blocking collectives  313 us (38%)
  other arithmetic  47.4 us (6%)
  matrix products  28 us (3%)
  local copies, waits for them, and re-layouts  21.7 us (3%)
  between operations  16.4 us (2%)
  loops' own time  10.8 us (1%)
    all_gather x1, waiting for transfers between devices, body(): lax.all_gather(xchan_input_weight, 'ctx', axis=0, tiled=True)  163 us
    all_gather x1, blocking collectives, prefix(): lax.all_gather(part.astype(kind), axis)  139 us
    ppermute x2, waiting for transfers between devices, doubled_up(): theirs = lax.ppermute(grown, axis, [(d, d ^ reach) for d in range(ways)])  89 us
    psum x4, waiting for transfers between devices, from_root(): return lax.psum(block, axis)  85.9 us
    all_gather x1, blocking collectives, body(): lax.all_gather(step_input_weight, 'ctx', axis=0, tiled=True)  73.3 us
    psum x4, blocking collectives, from_root(): return lax.psum(block, axis)  72.9 us
    reduce_scatter x1, waiting for transfers between devices, body(): lax.psum_scatter(term.astype(jnp.bfloat16), ('tp', 'dp'), scatter_dimensi...  24.5 us
    all_gather x1, waiting for transfers between devices, prefix(): lax.all_gather(part.astype(kind), axis)  21.9 us
  transfers between devices with their start and end apart: 12, of which 9 were waited for; matrix products, arithmetic and copies ran while one was open for 4% of the time, Pallas kernels for 0%

profile of v1, /device:TPU:0, one launch (start us, length us, event | category | flops | bytes accessed | tf_op | source)
XLA Modules:
  0.0 831.3 jit_solution(10547791710491602351)
XLA Ops:
  8.7 217.6 %while.37 = (s32[]{:T(128)}, bf16[1280,4,64]{0,2,1:T(8,128)(2,1)S(1)}, bf16[4,64,1024]{2,1,0:T(8,128)(2,1)S(1)}, bf16[4,64,128]{2,1,0:T(8,128)(2,1)S(1)}, bf16[1...) while((s32[]{:T(128)}, ...), condition=%wide.region_6.7_spmd, body=%wide.region_0.6_spmd.sunk | while | flops 606236 | bytes 5997076 | solution.py:178
  12.0 1.6 select_bitcast_fusion.4
  13.6 1.6 dynamic-slice_select_fusion.6
  15.2 1.6 select_bitcast_fusion.5
  16.7 1.6 dynamic-slice_select_fusion.7
  19.1 20.6 %psum.87 = bf16[1,64,128]{2,1,0:T(8,128)(2,1)S(1)} all-reduce(bf16[1,64,128]{2,1,0:T(8,128)(2,1)S(1)} %dynamic-slice_select_fusion.8), channel_id=1, replica_groups=mesh['groups'=2,'ctx'=4,'tp'=2,'dp'=2] {'ctx'}, use_global_device_ids=true, to_apply=%region_3.3 | all-reduce | flops 8192 | bytes 32768 | tf_op jit(solution)/shard_map/while/body/eval_jaxpr/psum | solution.py:24
  39.7 21.5 %all-reduce.5.cloned.1.call-done = (bf16[1280,1,64]{0,2,1:T(8,128)(2,1)}, bf16[1,64,1024]{2,1,0:T(8,128)(2,1)}, bf16[1024,1,64]{0,2,1:T(8,128)(2,1)}, bf16[1,64,1280]{2,1,0:T(8,128)(2,1)}) async-done(((bf16[1280,1,64]{0,2,1:T(8,128)(2,1)}, bf16[1,64,1024]{2,1,0:T(8,128)(2,1)}, bf16[1024,1,64]{0,2,1:T(8,128)(2,1)}, bf16[1,64,1280]{2,1,0:T(8,128)(2,1)}), (bf16[1280,1,64]{0,2,1:T(8,128)(2,1)}, ...) | async-done | bytes 589840 | tf_op jit(solution)/shard_map/while/body/eval_jaxpr/psum | solution.py:24
  63.0 1.6 constant_dynamic-update-slice_fusion.15
  68.8 1.6 select_bitcast_fusion.4
  70.4 1.6 dynamic-slice_select_fusion.6
  72.0 1.6 select_bitcast_fusion.5
  73.5 1.6 dynamic-slice_select_fusion.7
  75.9 17.5 %psum.87 = bf16[1,64,128]{2,1,0:T(8,128)(2,1)S(1)} all-reduce(bf16[1,64,128]{2,1,0:T(8,128)(2,1)S(1)} %dynamic-slice_select_fusion.8), channel_id=1, replica_groups=mesh['groups'=2,'ctx'=4,'tp'=2,'dp'=2] {'ctx'}, use_global_device_ids=true, to_apply=%region_3.3 | all-reduce | flops 8192 | bytes 32768 | tf_op jit(solution)/shard_map/while/body/eval_jaxpr/psum | solution.py:24
  93.3 21.4 %all-reduce.5.cloned.1.call-done = (bf16[1280,1,64]{0,2,1:T(8,128)(2,1)}, bf16[1,64,1024]{2,1,0:T(8,128)(2,1)}, bf16[1024,1,64]{0,2,1:T(8,128)(2,1)}, bf16[1,64,1280]{2,1,0:T(8,128)(2,1)}) async-done(((bf16[1280,1,64]{0,2,1:T(8,128)(2,1)}, bf16[1,64,1024]{2,1,0:T(8,128)(2,1)}, bf16[1024,1,64]{0,2,1:T(8,128)(2,1)}, bf16[1,64,1280]{2,1,0:T(8,128)(2,1)}), (bf16[1280,1,64]{0,2,1:T(8,128)(2,1)}, ...) | async-done | bytes 589840 | tf_op jit(solution)/shard_map/while/body/eval_jaxpr/psum | solution.py:24
  116.6 1.6 constant_dynamic-update-slice_fusion.15
  122.4 1.6 select_bitcast_fusion.4
  124.0 1.6 dynamic-slice_select_fusion.6
  125.6 1.6 select_bitcast_fusion.5
  127.1 1.6 dynamic-slice_select_fusion.7
  129.5 17.5 %psum.87 = bf16[1,64,128]{2,1,0:T(8,128)(2,1)S(1)} all-reduce(bf16[1,64,128]{2,1,0:T(8,128)(2,1)S(1)} %dynamic-slice_select_fusion.8), channel_id=1, replica_groups=mesh['groups'=2,'ctx'=4,'tp'=2,'dp'=2] {'ctx'}, use_global_device_ids=true, to_apply=%region_3.3 | all-reduce | flops 8192 | bytes 32768 | tf_op jit(solution)/shard_map/while/body/eval_jaxpr/psum | solution.py:24
  146.9 21.4 %all-reduce.5.cloned.1.call-done = (bf16[1280,1,64]{0,2,1:T(8,128)(2,1)}, bf16[1,64,1024]{2,1,0:T(8,128)(2,1)}, bf16[1024,1,64]{0,2,1:T(8,128)(2,1)}, bf16[1,64,1280]{2,1,0:T(8,128)(2,1)}) async-done(((bf16[1280,1,64]{0,2,1:T(8,128)(2,1)}, bf16[1,64,1024]{2,1,0:T(8,128)(2,1)}, bf16[1024,1,64]{0,2,1:T(8,128)(2,1)}, bf16[1,64,1280]{2,1,0:T(8,128)(2,1)}), (bf16[1280,1,64]{0,2,1:T(8,128)(2,1)}, ...) | async-done | bytes 589840 | tf_op jit(solution)/shard_map/while/body/eval_jaxpr/psum | solution.py:24
  170.2 1.6 constant_dynamic-update-slice_fusion.15
  176.0 1.6 select_bitcast_fusion.4
  177.6 1.6 dynamic-slice_select_fusion.6
  179.2 1.6 select_bitcast_fusion.5
  180.7 1.6 dynamic-slice_select_fusion.7
  183.1 17.5 %psum.87 = bf16[1,64,128]{2,1,0:T(8,128)(2,1)S(1)} all-reduce(bf16[1,64,128]{2,1,0:T(8,128)(2,1)S(1)} %dynamic-slice_select_fusion.8), channel_id=1, replica_groups=mesh['groups'=2,'ctx'=4,'tp'=2,'dp'=2] {'ctx'}, use_global_device_ids=true, to_apply=%region_3.3 | all-reduce | flops 8192 | bytes 32768 | tf_op jit(solution)/shard_map/while/body/eval_jaxpr/psum | solution.py:24
  200.5 21.4 %all-reduce.5.cloned.1.call-done = (bf16[1280,1,64]{0,2,1:T(8,128)(2,1)}, bf16[1,64,1024]{2,1,0:T(8,128)(2,1)}, bf16[1024,1,64]{0,2,1:T(8,128)(2,1)}, bf16[1,64,1280]{2,1,0:T(8,128)(2,1)}) async-done(((bf16[1280,1,64]{0,2,1:T(8,128)(2,1)}, bf16[1,64,1024]{2,1,0:T(8,128)(2,1)}, bf16[1024,1,64]{0,2,1:T(8,128)(2,1)}, bf16[1,64,1280]{2,1,0:T(8,128)(2,1)}), (bf16[1280,1,64]{0,2,1:T(8,128)(2,1)}, ...) | async-done | bytes 589840 | tf_op jit(solution)/shard_map/while/body/eval_jaxpr/psum | solution.py:24
  223.8 1.6 constant_dynamic-update-slice_fusion.15
  232.6 11.0 %psum.84 = bf16[128,64]{0,1:T(8,128)(2,1)S(1)} all-reduce(bf16[128,64]{0,1:T(8,128)(2,1)S(1)} %multiply_reduce_fusion.1), channel_id=1, replica_groups=mesh['groups'=2,'ctx'=4,'tp'=2,'dp'=2] {'tp','dp'}, use_global_device_ids=true, to_apply=%region_10.11 | all-reduce | flops 8192 | bytes 32768 | tf_op jit(solution)/shard_map/psum | solution.py:188
  243.6 73.3 %all_gather.29 = bf16[5120,16]{0,1:T(8,128)(2,1)S(1)} all-gather(bf16[1280,16]{0,1:T(8,128)(2,1)S(1)} %copy-done.4), channel_id=1, replica_groups=mesh['groups'=2,'ctx'=4,'tp'=2,'dp'=2] {'ctx'}, dimensions={0}, use_global_device_ids=true | all-gather | bytes 204800 | tf_op jit(solution)/shard_map/all_gather | solution.py:194
  318.3 1.9 compare_select_fusion
  320.6 2.2 convolution_add_fusion.1
  322.8 162.9 %all-gather.9.cloned.1.call-done = bf16[5120,1024]{1,0:T(8,128)(2,1)} async-done(((bf16[1280,1024]{1,0:T(8,128)(2,1)}), bf16[5120,1024]{1,0:T(8,128)(2,1)}) %all-gather.9.cloned.1.call-update) | async-done | bytes 10485776 | tf_op jit(solution)/shard_map/all_gather | solution.py:192
  485.8 5.6 convolution_add_fusion
  494.9 5.4 all_gather.28
  500.4 1.4 convolution_convert_fusion
  501.9 8.3 %maximum_select_fusion.4 = bf16[1024,2560]{1,0:T(8,128)(2,1)} fusion(bf16[1024,1280]{1,0:T(8,128)(2,1)} %collective-permute-done.1, bf16[1024,1280]{1,0:T(8,128)(2,1)} %param.36, pred[]{:T(512)S(6)} %eq.116), kind=kLoop, calls=%fused_computation.23 | loop fusion | flops 23592960 | bytes 10485761 | tf_op jit(solution)/shard_map/jit(_where)/select_n | solution.py:17
  510.2 3.5 collective-permute-start.2
  513.8 139.4 %all-gather.1 = bf16[4,1,16]{2,1,0:T(2,128)(2,1)S(1)} all-gather(bf16[1,1,16]{2,1,0:T(2,128)(2,1)S(1)} %get-tuple-element.473), channel_id=1, replica_groups=mesh['groups'=2,'ctx'=4,'tp'=2,'dp'=2] {'ctx'}, dimensions={0}, use_global_device_ids=true | all-gather | bytes 160 | tf_op jit(solution)/shard_map/all_gather | solution.py:36
  653.6 2.3 convolution_bitcast_fusion.1
  655.8 21.9 %all-gather.13.cloned.1.call-done = bf16[64,64,256]{2,1,0:T(8,128)(2,1)} async-done(((bf16[16,64,256]{2,1,0:T(8,128)(2,1)}), bf16[64,64,256]{2,1,0:T(8,128)(2,1)}) %all-gather.13.cloned.1.call-update) | async-done | bytes 2097168 | tf_op jit(solution)/shard_map/all_gather | solution.py:36
  677.8 5.4 while.38
  684.0 89.0 %collective-permute-done.2 = bf16[1024,2560]{1,0:T(8,128)(2,1)} collective-permute-done((bf16[1024,2560]{1,0:T(8,128)(2,1)}, bf16[1024,2560]{1,0:T(8,128)(2,1)}, u32[]{:S(2)}, u32[]{:S(2)}) %collective-permute-start.2) | collective-permute-done | bytes 5242912 | tf_op jit(solution)/shard_map/ppermute | solution.py:14
  773.1 12.5 %fusion.8 = bf16[128,5120]{1,0:T(8,128)(2,1)} fusion(bf16[128,1024]{0,1:T(8,128)(2,1)S(1)} %fusion.28, bf16[1024,2560]{1,0:T(8,128)(2,1)} %collective-permute-done.2, bf16[1024,2560]{1,0:T(8,128)(2,1)} %maximum_select_fusion.4, pred[]{:T(512)S(6)} %eq.115), kind=kOutput, calls=%fused_computation.22 | convolution fusion | flops 1390018560 | bytes 12058625 | tf_op jit(solution)/shard_map/dot_general | solution.py:246
  786.2 11.2 %psum.85 = bf16[128,64]{0,1:T(8,128)(2,1)S(1)} all-reduce(bf16[128,64]{0,1:T(8,128)(2,1)S(1)} %fusion.11), channel_id=1, replica_groups=mesh['groups'=2,'ctx'=4,'tp'=2,'dp'=2] {'tp','dp'}, use_global_device_ids=true, to_apply=%region_19.20 | all-reduce | flops 8192 | bytes 32768 | tf_op jit(solution)/shard_map/psum | solution.py:256
  797.6 24.5 %reduce-scatter.2.cloned.1.call-done = bf16[128,1280]{1,0:T(8,128)(2,1)} async-done(((bf16[128,5120]{1,0:T(8,128)(2,1)}), bf16[128,1280]{1,0:T(8,128)(2,1)}) %reduce-scatter.2.cloned.1.call-update) | async-done | bytes 327696 | tf_op jit(solution)/shard_map/reduce_scatter | solution.py:249
  822.2 1.8 add_convert_fusion
  (133 shorter events, 35.5 us)
Async XLA Ops:
  7.4 0.7 copy-start
  8.7 220.7 %copy-start.10 = (s32[4]{0:T(128)S(1)}, s32[4]{0:T(128)}, u32[]{:S(2)}) copy-start(s32[4]{0:T(128)} %param.24) | copy-start | bytes 52
  8.7 222.8 %copy-start.11 = (f32[16]{0:T(128)S(1)}, f32[16]{0:T(128)}, u32[]{:S(2)}) copy-start(f32[16]{0:T(128)} %param.33) | copy-start | bytes 196
  8.7 223.5 %copy-start.2 = (bf16[128,1280]{1,0:T(8,128)(2,1)S(1)}, bf16[128,1280]{1,0:T(8,128)(2,1)}, u32[]{:S(2)}) copy-start(bf16[128,1280]{1,0:T(8,128)(2,1)} %param.23) | copy-start | bytes 983044
  8.7 234.9 %copy-start.4 = (bf16[1280,16]{0,1:T(8,128)(2,1)S(1)}, bf16[1280,16]{0,1:T(8,128)(2,1)}, u32[]{:S(2)}) copy-start(bf16[1280,16]{0,1:T(8,128)(2,1)} %param.29) | copy-start | bytes 122884
  8.7 308.2 %copy-start.6 = (f32[4,1024]{1,0:T(4,128)S(1)}, f32[4,1024]{1,0:T(4,128)}, u32[]{:S(2)}) copy-start(f32[4,1024]{1,0:T(4,128)} %param.30) | copy-start | bytes 49156
  8.7 308.2 %copy-start.7 = (f32[4,128]{1,0:T(4,128)S(1)}, f32[4,128]{1,0:T(4,128)}, u32[]{:S(2)}) copy-start(f32[4,128]{1,0:T(4,128)} %param.31) | copy-start | bytes 6148
  8.8 52.4 %all-reduce.5.cloned.1.call-start = ((), (), s32[]{:S(2)}) async-start(), calls=%async_computation.6 | async-start | bytes 1179648 | tf_op jit(solution)/shard_map/while/body/eval_jaxpr/psum | solution.py:24
  65.6 49.2 %all-reduce.5.cloned.1.call-start = ((), (), s32[]{:S(2)}) async-start(), calls=%async_computation.6 | async-start | bytes 1179648 | tf_op jit(solution)/shard_map/while/body/eval_jaxpr/psum | solution.py:24
  119.2 49.2 %all-reduce.5.cloned.1.call-start = ((), (), s32[]{:S(2)}) async-start(), calls=%async_computation.6 | async-start | bytes 1179648 | tf_op jit(solution)/shard_map/while/body/eval_jaxpr/psum | solution.py:24
  172.7 49.2 %all-reduce.5.cloned.1.call-start = ((), (), s32[]{:S(2)}) async-start(), calls=%async_computation.6 | async-start | bytes 1179648 | tf_op jit(solution)/shard_map/while/body/eval_jaxpr/psum | solution.py:24
  226.3 92.0 %copy-start.8 = (f32[16]{0:T(128)S(1)}, f32[16]{0:T(128)}, u32[]{:S(2)}) copy-start(f32[16]{0:T(128)} %param.32) | copy-start | bytes 196
  226.3 91.9 %all-gather.7.cloned.1.call-start = ((), (), s32[]{:S(2)}) async-start(), calls=%async_computation.1 | async-start | bytes 1638400 | tf_op jit(solution)/shard_map/all_gather | solution.py:190
  226.9 93.7 %all-gather.11.cloned.1.call-start = ((), (), s32[]{:S(2)}) async-start(), calls=%async_computation.3 | async-start | bytes 1638400 | tf_op jit(solution)/shard_map/all_gather | solution.py:193
  227.5 258.2 %all-gather.9.cloned.1.call-start = ((), (), s32[]{:S(2)}) async-start(), calls=%async_computation.2 | async-start | bytes 13107200 | tf_op jit(solution)/shard_map/all_gather | solution.py:192
  228.1 449.7 %all-gather.13.cloned.1.call-start = ((), (), s32[]{:S(2)}) async-start(), calls=%async_computation.5 | async-start | bytes 2621440 | tf_op jit(solution)/shard_map/all_gather | solution.py:36
  228.1 273.7 %collective-permute-start.1 = (bf16[1024,1280]{1,0:T(8,128)(2,1)}, bf16[1024,1280]{1,0:T(8,128)(2,1)}, u32[]{:S(2)}, u32[]{:S(2)}) collective-permute-start(bf16[1024,1280]{1,0:T(8,128)(2,1)} %param.36), channel_id=1, source_target_pairs={{0,4},{4,0},{8,12},{12,8},{1,5},{5,1},{9,13},{13,9},{2,6},{6,2},{1... | collective-permute-start | bytes 7864328 | tf_op jit(solution)/shard_map/ppermute | solution.py:14
  318.3 167.5 %copy-start.1 = (bf16[128,5120]{1,0:T(8,128)(2,1)S(1)}, bf16[128,5120]{1,0:T(8,128)(2,1)}, u32[]{:S(2)}) copy-start(bf16[128,5120]{1,0:T(8,128)(2,1)} %all-gather.7.cloned.1.call-done) | copy-start | bytes 3932164
  491.4 2.7 collective-permute-start
  501.8 320.4 %reduce-scatter.2.cloned.1.call-start = ((), (), s32[]{:S(2)}) async-start(), calls=%async_computation.4 | async-start | bytes 1638400 | tf_op jit(solution)/shard_map/reduce_scatter | solution.py:249
  510.2 262.9 %collective-permute-start.2 = (bf16[1024,2560]{1,0:T(8,128)(2,1)}, bf16[1024,2560]{1,0:T(8,128)(2,1)}, u32[]{:S(2)}, u32[]{:S(2)}) collective-permute-start(bf16[1024,2560]{1,0:T(8,128)(2,1)} %maximum_select_fusion.4), channel_id=1, source_target_pairs={{0,8},{4,12},{8,0},{12,4},{1,9},{5,13},{9,1},{13,5},{2,10},{6,14},... | collective-permute-start | bytes 15728648 | tf_op jit(solution)/shard_map/ppermute | solution.py:14
  677.8 5.4 copy-start.9
  677.8 6.1 copy-start.5
  684.0 101.8 %copy-start.3 = (bf16[1024,4,64]{0,2,1:T(8,128)(2,1)S(1)}, bf16[1024,4,64]{0,2,1:T(8,128)(2,1)}, u32[]{:S(2)}) copy-start(bf16[1024,4,64]{0,2,1:T(8,128)(2,1)} %get-tuple-element.396) | copy-start | bytes 1572868
Sparse Core Ops, SparseCore 0:
  18.5 42.6 all-reduce.4
  75.3 39.4 all-reduce.4
  128.9 39.4 all-reduce.4
  182.5 39.4 all-reduce.4
Sparse Core Ops, SparseCore 1:
  228.4 17.6 all-gather.6
  247.5 50.3 all-gather.10
  299.3 186.4 all-gather.8
  501.9 175.8 all-gather.12
  785.7 36.4 reduce-scatter.1
